TPU v7x, 32 devices: a whole 2x2x4 slice. The times are simulated.
32 devices in a mesh: seq: 8 (over y, x, core), head: 4 (over z).
Axes of the slice: x: 2, y: 2, z: 4, core: 2. Of those that a mesh axis runs over, the one named last changes fastest.
Arguments:
- tokens: bfloat16 [4096, 5376], P('seq', 'head'), may hold values from -32 to 32
- query_weight: bfloat16 [5376, 4096], P(None, 'head'), may hold values from -1 to 1
- key_weight: bfloat16 [5376, 2048], P(None, 'head'), may hold values from -1 to 1
- value_weight: bfloat16 [5376, 2048], P(None, 'head'), may hold values from -0.078125 to 0.078125
- output_grad: bfloat16 [4096, 4096], P('seq', 'head'), may hold values from -48 to 48
- segments: int32 [4096], replicated, may hold values from 0 to 3, never falling along the last dimension, each value on 1 to 2048 neighbouring positions
Outputs:
- token_grad: bfloat16 [4096, 5376], P('seq', 'head')
- query_weight_grad: bfloat16 [5376, 4096], P('seq', 'head')
- key_weight_grad: bfloat16 [5376, 2048], P('seq', 'head')
- value_weight_grad: bfloat16 [5376, 2048], P('seq', 'head')
Inputs may be any that keep to these rules, and one draw needn't show every extreme that they name: `segments`: segment numbers never fall along the tokens; a segment has at most 2048 tokens.
All inputs are finite; a program needn't handle non-finite values.
Results may differ from a plain program's by a relative error of at most 0.015.
The roundings to bfloat16 on the way count: a program that leaves them out, or rounds other values in their place, can miss the bound.
Values may be sent and summed in bfloat16 or wider, within the bound.
No kernel may reach another device: no remote copies, remote signals or barrier semaphores. Data moves between devices by JAX's collectives and lax.ppermute only.
A program may use at most 192 MiB of HBM per device.

v0:
```python
import jax
import jax.numpy as jnp
from jax import lax
from jax.sharding import PartitionSpec as P

D = 5376
HEADS = 32
KV_HEADS = 16
HEAD_DIM = 128
WINDOW = 1024
HOPS = 2
neg_large = -1e30


def passed_along(x, axis, by):
    count = lax.axis_size(axis)
    pairs = [(i, i + by) for i in range(count) if 0 <= i + by < count]
    return lax.ppermute(x, axis, pairs)


def contract_last(left, right):
    return lax.dot_general(
        left, right, (((1,), (1,)), ((), ())), preferred_element_type=jnp.float32
    )


def contract_first(left, right):
    return lax.dot_general(
        left, right, (((0,), (0,)), ((), ())), preferred_element_type=jnp.float32
    )


def attend(queries, key_value, grads, query_first, key_first, seg_query, seg_key):
    tok_rows = queries.shape[0]
    key_rows = key_value.shape[1]
    groups = HEADS // KV_HEADS
    kv_local = key_value.shape[2] // HEAD_DIM
    score_scale = (D / HEADS) ** (-0.5)
    query_four = queries.reshape(tok_rows, kv_local, groups, HEAD_DIM)
    grad_four = grads.reshape(tok_rows, kv_local, groups, HEAD_DIM)
    key_three = key_value[0].reshape(key_rows, kv_local, HEAD_DIM)
    value_three = key_value[1].reshape(key_rows, kv_local, HEAD_DIM)
    query_pos = query_first + jnp.arange(tok_rows, dtype=jnp.int32)
    key_pos = key_first + jnp.arange(key_rows, dtype=jnp.int32)
    spacing = query_pos[:, None] - key_pos[None, :]
    allowed = (
        (key_pos >= 0)[None, :]
        & (spacing >= 0)
        & (spacing < WINDOW)
        & (seg_query[:, None] == seg_key[None, :])
    )
    scores = (
        jnp.einsum("akgd,ckd->kgac", query_four, key_three, preferred_element_type=jnp.float32)
        * score_scale
    )
    masked = jnp.where(allowed, scores, neg_large)
    row_max = jnp.max(masked, axis=-1, keepdims=True)
    expo = jnp.where(allowed, jnp.exp(masked - row_max), 0.0)
    probs = expo / jnp.sum(expo, axis=-1, keepdims=True)
    dprobs = jnp.einsum(
        "akgd,ckd->kgac", grad_four, value_three, preferred_element_type=jnp.float32
    )
    center = jnp.sum(probs * dprobs, axis=-1, keepdims=True)
    dscores = (probs * (dprobs - center)).astype(jnp.bfloat16)
    probs_low = probs.astype(jnp.bfloat16)
    query_grad = (
        (
            jnp.einsum("kgac,ckd->akgd", dscores, key_three, preferred_element_type=jnp.float32)
            * score_scale
        )
        .reshape(tok_rows, -1)
        .astype(jnp.bfloat16)
    )
    key_grad = (
        jnp.einsum("kgac,akgd->ckd", dscores, query_four, preferred_element_type=jnp.float32)
        * score_scale
    ).reshape(key_rows, -1)
    value_grad = jnp.einsum(
        "kgac,akgd->ckd", probs_low, grad_four, preferred_element_type=jnp.float32
    ).reshape(key_rows, -1)
    return (query_grad, jnp.stack([key_grad, value_grad]))


def per_device(tokens, query_weight, key_weight, value_weight, output_grad, segments):
    tok_rows = tokens.shape[0]
    hop_count = HOPS
    margin = hop_count * tok_rows
    gathered = lax.all_gather(tokens, "head", axis=1, tiled=True)
    queries = jnp.dot(gathered, query_weight, preferred_element_type=jnp.float32).astype(
        jnp.bfloat16
    )
    keys_own = jnp.dot(gathered, key_weight, preferred_element_type=jnp.float32).astype(
        jnp.bfloat16
    )
    values_own = jnp.dot(gathered, value_weight, preferred_element_type=jnp.float32).astype(
        jnp.bfloat16
    )
    key_value = jnp.stack([keys_own, values_own])
    blocks = [key_value] * (hop_count + 1)
    moving = key_value
    for distance in range(1, hop_count + 1):
        moving = passed_along(moving, "seq", 1)
        blocks[hop_count - distance] = moving
    keys_all = jnp.concatenate(blocks, axis=1)
    position = lax.axis_index("seq")
    query_first = position * tok_rows
    seg_query = lax.dynamic_slice_in_dim(segments, query_first, tok_rows, 0)
    seg_padded = jnp.concatenate([jnp.full((margin,), -1, jnp.int32), segments], axis=0)
    seg_key = lax.dynamic_slice_in_dim(seg_padded, query_first, (hop_count + 1) * tok_rows, 0)
    query_grad, kv_grad = attend(
        queries, keys_all, output_grad, query_first, query_first - margin, seg_query, seg_key
    )
    pieces = [
        kv_grad[:, block * tok_rows : (block + 1) * tok_rows] for block in range(hop_count + 1)
    ]
    carried = pieces[0]
    for distance in range(1, hop_count + 1):
        carried = pieces[distance] + passed_along(carried.astype(jnp.bfloat16), "seq", -1).astype(
            carried.dtype
        )
    key_grad = carried[0].astype(jnp.bfloat16)
    value_grad = carried[1].astype(jnp.bfloat16)
    partial_term = (
        contract_last(query_grad, query_weight)
        + contract_last(key_grad, key_weight)
        + contract_last(value_grad, value_weight)
    )
    token_grad = lax.psum_scatter(
        partial_term.astype(jnp.bfloat16), "head", scatter_dimension=1, tiled=True
    )
    proj_grads = jnp.concatenate([query_grad, key_grad, value_grad], axis=1)
    summed = lax.psum_scatter(
        contract_first(gathered, proj_grads).astype(jnp.bfloat16),
        "seq",
        scatter_dimension=0,
        tiled=True,
    ).astype(jnp.float32)
    summed = summed * (tok_rows * lax.axis_size("seq")) ** (-0.5)
    q_width = query_weight.shape[1]
    k_width = key_weight.shape[1]
    query_weight_grad = summed[:, :q_width].astype(jnp.bfloat16)
    key_weight_grad = summed[:, q_width : q_width + k_width].astype(jnp.bfloat16)
    value_weight_grad = summed[:, q_width + k_width :].astype(jnp.bfloat16)
    return (token_grad, query_weight_grad, key_weight_grad, value_weight_grad)


def solution(mesh):
    in_specs = (
        P("seq", "head"),
        P(None, "head"),
        P(None, "head"),
        P(None, "head"),
        P("seq", "head"),
        P(),
    )
    out_specs = (P("seq", "head"), P("seq", "head"), P("seq", "head"), P("seq", "head"))
    return jax.shard_map(
        per_device, mesh=mesh, in_specs=in_specs, out_specs=out_specs, check_vma=False
    )
```

profile of v0, /device:TPU:0, one launch (start us, length us, event | category | flops | bytes accessed | tf_op | source)
XLA Modules:
  0.0 569.0 jit_solution(12160398720478876539)
XLA Ops:
  7.2 0.7 all-gather.2.cloned.1.call-update
  7.9 0.0 reduce-scatter.7.cloned.1.call-start
  7.9 106.7 %all-gather.2.cloned.1.call-done = bf16[512,5376]{0,1:T(8,128)(2,1)} async-done(((bf16[512,1344]{0,1:T(8,128)(2,1)}), bf16[512,5376]{0,1:T(8,128)(2,1)}) %all-gather.2.cloned.1.call-update) | async-done | bytes 5505040 | tf_op jit(solution)/shard_map/all_gather | solution.py:88
  114.7 7.3 %fusion.32 = bf16[1,512,512]{2,1,0:T(8,128)(2,1)S(1)} fusion(bf16[512,5376]{0,1:T(8,128)(2,1)} %all-gather.2.cloned.1.call-done, bf16[5376,512]{1,0:T(8,128)(2,1)} %param.9), kind=kOutput, calls=%fused_computation.52 | convolution fusion | flops 2818834432 | bytes 11534336 | tf_op jit(solution)/shard_map/dot_general | solution.py:95
  122.1 5.7 fusion.31
  127.8 0.1 pad_maximum_fusion.1
  127.9 2.9 collective-permute-start
  130.8 1.3 copy.53
  132.1 0.1 dynamic_slice.6
  132.2 0.1 pad_dynamic-slice_fusion
  132.3 2.6 fusion.16
  134.9 10.3 %collective-permute-start.1 = (bf16[2,512,512]{2,1,0:T(8,128)(2,1)}, bf16[2,512,512]{2,1,0:T(8,128)(2,1)S(1)}, u32[]{:S(2)}, u32[]{:S(2)}) collective-permute-start(bf16[2,512,512]{2,1,0:T(8,128)(2,1)} %collective-permute-done), channel_id=1, source_target_pairs={{0,4},{4,8},{8,12},{12,16},{16,20},{20,24},{24,28},{1,5},{5,9},{9,... | collective-permute-start | bytes 3145736 | tf_op jit(solution)/shard_map/ppermute | solution.py:18
  145.2 10.4 %convolution_convert_fusion.1 = bf16[512,1024]{1,0:T(8,128)(2,1)S(1)} fusion(bf16[512,5376]{0,1:T(8,128)(2,1)} %all-gather.2.cloned.1.call-done, bf16[5376,1024]{1,0:T(8,128)(2,1)} %param.7), kind=kOutput, calls=%fused_computation.48 | convolution fusion | flops 5637668864 | bytes 17563648 | tf_op jit(solution)/shard_map/dot_general | solution.py:89
  155.6 1.3 copy.52
  156.9 1.4 maximum_maximum_fusion
  158.3 1.4 fusion.38
  159.7 0.4 reshape_squeeze.6
  160.1 1.0 copy.38
  161.1 2.8 reshape_squeeze.7
  163.9 17.4 %fusion.39 = (f32[4,2,512]{2,1,0:T(2,128)S(1)}, f32[4,2,512,1536]{2,3,1,0:T(8,128)}) fusion(pred[512,1536]{0,1:T(8,128)(4,1)} %fusion.16, bf16[1536,4,128,1]{0,2,3,1:T(8,128)(2,1)S(1)} %copy.38, bf16[512,4,2,128]{0,3,2,1:T(8,128)(2,1)} %bitcast.77), kind=kOutput, calls=%fused_computation.66 | convolution fusion | flops 1642071552 | bytes 28590080 | tf_op jit(solution)/shard_map/sub | solution.py:58
  181.3 12.5 %fusion.6 = f32[4,1536,128,1]{1,2,3,0:T(8,128)} fusion(bf16[512,4,2,128]{0,3,2,1:T(8,128)(2,1)} %bitcast.80, f32[4,2,512,1536]{2,3,1,0:T(8,128)} %get-tuple-element.19, f32[4,2,512]{2,1,0:T(2,128)S(1)} %get-tuple-element.18), kind=kOutput, calls=%fused_computation.11 | convolution fusion | flops 1623195648 | bytes 29376512 | tf_op jit(solution)/shard_map/kgac,akgd->ckd/dot_general | solution.py:78
  193.8 16.6 %fusion.1 = (f32[4,2,512]{2,1,0:T(2,128)S(1)}, f32[4,1536,512,2]{2,1,3,0:T(8,128)}) fusion(f32[4,2,512,1536]{2,3,1,0:T(8,128)} %get-tuple-element.19, f32[4,2,512]{2,1,0:T(2,128)S(1)} %get-tuple-element.18, bf16[512,4,2,128]{0,3,2,1:T(8,128)(2,1)S(1)} %bitcast.81, bf16[1536,4,128,1]{2,1,0,3:T(4,128)(2,1)S(1)} %bitcast.79), kind=kOutput, calls=%fused_computation.3 | convolution fusion | flops 1629483008 | bytes 52985856 | tf_op jit(solution)/shard_map/akgd,ckd->kgac/dot_general | solution.py:60
  210.4 16.8 %fusion.3 = bf16[4,2,512,1536]{2,3,1,0:T(8,128)(2,1)S(1)} fusion(f32[4,1536,512,2]{2,1,3,0:T(8,128)} %get-tuple-element.21, f32[4,2,512]{2,1,0:T(2,128)S(1)} %get-tuple-element.20, f32[4,2,512,1536]{2,3,1,0:T(8,128)} %get-tuple-element.19, f32[4,2,512]{2,1,0:T(2,128)S(1)} %get-tuple-element.18), kind=kLoop, calls=%fused_computation.5 | loop fusion | flops 25165824 | bytes 62947328 | tf_op jit(solution)/shard_map/convert_element_type | solution.py:64
  227.2 7.0 %fusion.13 = f32[4,128,1536]{2,1,0:T(8,128)} fusion(bf16[512,4,2,128]{0,3,2,1:T(8,128)(2,1)} %bitcast.78, bf16[4,2,512,1536]{2,3,1,0:T(8,128)(2,1)S(1)} %fusion.3), kind=kOutput, calls=%fused_computation.27 | convolution fusion | flops 1611399168 | bytes 16777216 | tf_op jit(solution)/shard_map/kgac,akgd->ckd/dot_general | solution.py:75
  234.2 1.8 fusion.23
  236.1 1.6 collective-permute-start.2
  237.7 5.4 collective-permute-done.2
  243.1 0.4 fusion.19
  243.5 1.3 collective-permute-start.3
  244.8 2.8 multiply_convert_fusion.1
  247.6 12.7 %collective-permute-done.3 = bf16[2,512,512]{1,2,0:T(8,128)(2,1)S(1)} collective-permute-done((bf16[2,512,512]{1,2,0:T(8,128)(2,1)S(1)}, bf16[2,512,512]{1,2,0:T(8,128)(2,1)S(1)}, u32[]{:S(2)}, u32[]{:S(2)}) %collective-permute-start.3) | collective-permute-done | bytes 1048608 | tf_op jit(solution)/shard_map/ppermute | solution.py:18
  260.2 0.4 fusion.22
  260.6 0.1 slice_bitcast_fusion.1
  260.7 20.0 %fusion.5 = bf16[5376,2048]{0,1:T(8,128)(2,1)} fusion(bf16[512,5376]{0,1:T(8,128)(2,1)} %all-gather.2.cloned.1.call-done, bf16[512,512]{0,1:T(8,128)(2,1)S(1)} %get-tuple-element.17, bf16[512,512]{0,1:T(8,128)(2,1)S(1)} %get-tuple-element.16, bf16[512,1024]{0,1:T(8,128)(2,1)S(1)} %bitcast.82), kind=kOutput, calls=%fused_computation.10 | convolution fusion | flops 11291590656 | bytes 29622272 | tf_op jit(solution)/shard_map/dot_general | solution.py:28
  280.7 28.2 %copy.50 = bf16[5376,2048]{1,0:T(8,128)(2,1)} copy(bf16[5376,2048]{0,1:T(8,128)(2,1)} %fusion.5) | data formatting | bytes 44040192
  308.9 0.0 reduce-scatter.5.cloned.1.call-start
  309.0 13.0 %fusion.40 = f32[512,5376]{0,1:T(8,128)} fusion(bf16[5376,1024]{1,0:T(8,128)(2,1)} %param.7, bf16[512,1024]{0,1:T(8,128)(2,1)S(1)} %bitcast.83), kind=kOutput, calls=%fused_computation.67 | convolution fusion | flops 5637144576 | bytes 23068672 | tf_op jit(solution)/shard_map/dot_general | solution.py:22
  321.9 9.3 %fusion.36 = f32[512,5376]{0,1:T(8,128)} fusion(bf16[5376,512]{1,0:T(8,128)(2,1)} %param.8, bf16[2,512,512]{1,2,0:T(8,128)(2,1)S(1)} %fusion.22), kind=kOutput, calls=%fused_computation.63 | convolution fusion | flops 2818572288 | bytes 17039360 | tf_op jit(solution)/shard_map/dot_general | solution.py:22
  331.3 19.3 %add_convert_fusion = bf16[512,5376]{0,1:T(8,128)(2,1)} fusion(f32[512,5376]{0,1:T(8,128)} %fusion.40, f32[512,5376]{0,1:T(8,128)} %fusion.36, bf16[5376,512]{1,0:T(8,128)(2,1)} %param.9, bf16[2,512,512]{1,2,0:T(8,128)(2,1)S(1)} %fusion.22), kind=kOutput, calls=%fused_computation.17 | convolution fusion | flops 2826829824 | bytes 33554432 | tf_op jit(solution)/shard_map/dot_general | solution.py:22
  350.6 111.0 %reduce-scatter.7.cloned.1.call-done = bf16[672,2048]{1,0:T(8,128)(2,1)} async-done(((bf16[5376,2048]{1,0:T(8,128)(2,1)}), bf16[672,2048]{1,0:T(8,128)(2,1)}) %reduce-scatter.7.cloned.1.call-update) | async-done | bytes 2752528
  461.6 4.6 copy.51
  466.2 2.5 multiply_convert_fusion
  468.7 1.3 slice.54
  469.9 2.9 copy.33
  472.9 1.3 fusion.37
  474.1 2.2 copy.34
  476.4 2.2 copy.35
  478.6 83.9 %reduce-scatter.5.cloned.1.call-done = bf16[512,1344]{0,1:T(8,128)(2,1)} async-done(((bf16[512,5376]{0,1:T(8,128)(2,1)}), bf16[512,1344]{0,1:T(8,128)(2,1)}) %reduce-scatter.5.cloned.1.call-update) | async-done | bytes 1376272 | tf_op jit(solution)/shard_map/reduce_scatter | solution.py:128
  (25 shorter events, 0.1 us)
Async XLA Ops:
  7.2 107.5 %all-gather.2.cloned.1.call-start = ((), (), s32[]{:S(2)}) async-start(), calls=%async_computation.2 | async-start | bytes 6881280 | tf_op jit(solution)/shard_map/all_gather | solution.py:88
  7.9 453.7 %reduce-scatter.7.cloned.1.call-start = ((), (), s32[]{:S(2)}) async-start(), calls=%async_computation.4 | async-start | bytes 24772608
  114.7 7.4 %copy-start.8 = (bf16[512,5376]{0,1:T(8,128)(2,1)S(1)}, bf16[512,5376]{0,1:T(8,128)(2,1)}, u32[]{:S(2)}) copy-start(bf16[512,5376]{0,1:T(8,128)(2,1)} %all-gather.2.cloned.1.call-done) | copy-start | bytes 16515076
  122.1 8.7 %copy-start.4 = (bf16[512,1024]{1,0:T(8,128)(2,1)S(1)}, bf16[512,1024]{1,0:T(8,128)(2,1)}, u32[]{:S(2)}) copy-start(bf16[512,1024]{1,0:T(8,128)(2,1)} %param.10) | copy-start | bytes 3145732
  122.1 10.0 %copy-start.7 = (s32[4096]{0:T(1024)S(1)}, s32[4096]{0:T(1024)}, u32[]{:S(2)}) copy-start(s32[4096]{0:T(1024)} %param.11) | copy-start | bytes 49156
  127.9 7.0 %collective-permute-start = (bf16[2,512,512]{2,1,0:T(8,128)(2,1)S(1)}, bf16[2,512,512]{2,1,0:T(8,128)(2,1)}, u32[]{:S(2)}, u32[]{:S(2)}) collective-permute-start(bf16[2,512,512]{2,1,0:T(8,128)(2,1)S(1)} %pad_maximum_fusion.1), channel_id=1, source_target_pairs={{0,4},{4,8},{8,12},{12,16},{16,20},{20,24},{24,28},{1,5},{5,9},{9,... | collective-permute-start | bytes 3145736 | tf_op jit(solution)/shard_map/ppermute | solution.py:18
  134.9 22.0 %collective-permute-start.1 = (bf16[2,512,512]{2,1,0:T(8,128)(2,1)}, bf16[2,512,512]{2,1,0:T(8,128)(2,1)S(1)}, u32[]{:S(2)}, u32[]{:S(2)}) collective-permute-start(bf16[2,512,512]{2,1,0:T(8,128)(2,1)} %collective-permute-done), channel_id=1, source_target_pairs={{0,4},{4,8},{8,12},{12,16},{16,20},{20,24},{24,28},{1,5},{5,9},{9,... | collective-permute-start | bytes 3145736 | tf_op jit(solution)/shard_map/ppermute | solution.py:18
  161.1 20.2 %copy-start.2 = (bf16[1536,4,128,1]{0,2,3,1:T(8,128)(2,1)}, bf16[1536,4,128,1]{0,2,3,1:T(8,128)(2,1)S(1)}, u32[]{:S(2)}) copy-start(bf16[1536,4,128,1]{0,2,3,1:T(8,128)(2,1)S(1)} %copy.38) | copy-start | bytes 4718596
  181.3 12.5 %copy-start.5 = (bf16[512,1024]{0,1:T(8,128)(2,1)S(1)}, bf16[512,1024]{0,1:T(8,128)(2,1)}, u32[]{:S(2)}) copy-start(bf16[512,1024]{0,1:T(8,128)(2,1)} %copy.53) | copy-start | bytes 3145732
  234.2 8.9 %copy-start = (f32[4,128,1536]{2,1,0:T(8,128)S(1)}, f32[4,128,1536]{2,1,0:T(8,128)}, u32[]{:S(2)}) copy-start(f32[4,128,1536]{2,1,0:T(8,128)} %fusion.13) | copy-start | bytes 9437188
  234.2 8.9 %copy-start.1 = (f32[4,1536,128,1]{1,2,3,0:T(8,128)S(1)}, f32[4,1536,128,1]{1,2,3,0:T(8,128)}, u32[]{:S(2)}) copy-start(f32[4,1536,128,1]{1,2,3,0:T(8,128)} %fusion.6) | copy-start | bytes 9437188
  236.1 8.7 %copy-start.3 = (bf16[1536,4,128,1]{0,2,3,1:T(8,128)(2,1)S(1)}, bf16[1536,4,128,1]{0,2,3,1:T(8,128)(2,1)}, u32[]{:S(2)}) copy-start(bf16[1536,4,128,1]{0,2,3,1:T(8,128)(2,1)} %copy-done.2) | copy-start | bytes 4718596
  236.1 7.0 %collective-permute-start.2 = (bf16[2,512,512]{1,2,0:T(8,128)(2,1)S(1)}, bf16[2,512,512]{1,2,0:T(8,128)(2,1)S(1)}, u32[]{:S(2)}, u32[]{:S(2)}) collective-permute-start(bf16[2,512,512]{1,2,0:T(8,128)(2,1)S(1)} %fusion.23), channel_id=1, source_target_pairs={{4,0},{8,4},{12,8},{16,12},{20,16},{24,20},{28,24},{5,1},{9,5},{13... | collective-permute-start | bytes 3145736 | tf_op jit(solution)/shard_map/ppermute | solution.py:18
  243.5 16.8 %collective-permute-start.3 = (bf16[2,512,512]{1,2,0:T(8,128)(2,1)S(1)}, bf16[2,512,512]{1,2,0:T(8,128)(2,1)S(1)}, u32[]{:S(2)}, u32[]{:S(2)}) collective-permute-start(bf16[2,512,512]{1,2,0:T(8,128)(2,1)S(1)} %fusion.19), channel_id=1, source_target_pairs={{4,0},{8,4},{12,8},{16,12},{20,16},{24,20},{28,24},{5,1},{9,5},{13... | collective-permute-start | bytes 3145736 | tf_op jit(solution)/shard_map/ppermute | solution.py:18
  247.6 13.1 %copy-start.6 = (bf16[4,128,2,512]{3,1,2,0:T(8,128)(2,1)S(1)}, bf16[4,128,2,512]{3,1,2,0:T(8,128)(2,1)}, u32[]{:S(2)}) copy-start(bf16[4,128,2,512]{3,1,2,0:T(8,128)(2,1)} %multiply_convert_fusion.1) | copy-start | bytes 3145732
  308.9 253.6 %reduce-scatter.5.cloned.1.call-start = ((), (), s32[]{:S(2)}) async-start(), calls=%async_computation.3 | async-start | bytes 6881280 | tf_op jit(solution)/shard_map/reduce_scatter | solution.py:128
Sparse Core Ops, SparseCore 0:
  9.6 105.0 all-gather.1
  309.0 152.5 reduce-scatter.6
  464.5 97.9 reduce-scatter.4
where the time goes:
time: 570 us; the launch traced here: 569 us
  waiting for transfers between devices  320 us (56%)
  matrix products  141 us (25%)
  local copies, waits for them, and re-layouts  51.1 us (9%)
  other arithmetic  26 us (5%)
  starting transfers between devices  16.2 us (3%)
  between operations  14 us (2%)
    unnamed x4, waiting for transfers between devices  112 us
    all_gather x1, waiting for transfers between devices, per_device(): gathered = lax.all_gather(tokens, 'head', axis=1, tiled=True)  107 us
    reduce_scatter x1, waiting for transfers between devices, per_device(): lax.psum_scatter(partial_term.astype(jnp.bfloat16), 'head', scatter_dimen...  83.9 us
    dot_general x3, matrix products, contract_last(): lax.dot_general(left, right, (((1,), (1,)), ((), ())), preferred_element_...  41.6 us
    unnamed x23, local copies, waits for them, and re-layouts  40.2 us
    dot_general x1, matrix products, contract_first(): lax.dot_general(left, right, (((0,), (0,)), ((), ())), preferred_element_...  20 us
    ppermute x4, waiting for transfers between devices, passed_along(): return lax.ppermute(x, axis, pairs)  18.1 us
    sub x1, matrix products, attend(): expo = jnp.where(allowed, jnp.exp(masked - row_max), 0.0)  17.4 us
  transfers between devices with their start and end apart: 7, of which 5 were waited for; matrix products, arithmetic and copies ran while one was open for 14% of the time, Pallas kernels for 0%

commit v1 on v0

--- a/solution.py
+++ b/solution.py
@@ -85,7 +85,12 @@
     tok_rows = tokens.shape[0]
     hop_count = HOPS
     margin = hop_count * tok_rows
-    gathered = lax.all_gather(tokens, "head", axis=1, tiled=True)
+    ring = [tokens]
+    for hop in range(3):
+        ring.append(lax.ppermute(ring[-1], "head", [(dev, (dev + 1) % 4) for dev in range(4)]))
+    gathered = jnp.roll(
+        jnp.concatenate(ring[::-1], axis=1), (lax.axis_index("head") + 1) * ring[0].shape[1], axis=1
+    )
     queries = jnp.dot(gathered, query_weight, preferred_element_type=jnp.float32).astype(
         jnp.bfloat16
     )

time: 570 us -> 544 us (0.954)
  local copies, waits for them, and re-layouts: 51.1 us -> 19.8 us
    unnamed x4 -> x2, waiting for transfers between devices: 112 us -> 0.03 us
    reduce_scatter x0 -> x1, waiting for transfers between devices: none -> 111 us  [per_device(): lax.psum_scatter(contract_first(gathered, proj_grads).astype(jnp.bfloat16...]
    all_gather x1 -> x0, waiting for transfers between devices: 107 us -> none  [per_device(): gathered = lax.all_gather(tokens, 'head', axis=1, tiled=True)]
    ppermute x0 -> x3, waiting for transfers between devices: none -> 98.2 us  [per_device(): lax.ppermute(ring[-1], 'head', [(dev, (dev + 1) % 4) for dev in range(4)])]
    unnamed x23 -> x35, local copies, waits for them, and re-layouts: 40.2 us -> 8.93 us
    reduce_scatter x1, waiting for transfers between devices: 83.9 us -> 96.1 us  [per_device(): lax.psum_scatter(partial_term.astype(jnp.bfloat16), 'head', scatter_dimen...]
  transfers between devices with their start and end apart: 7 -> 9, of which waited for: 5 -> 7; matrix products, arithmetic and copies ran while one was open for 14% -> 12% of each run, Pallas kernels for 0% -> 0%
where the time goes in v1:
time: 544 us; the launch traced here: 537 us
  waiting for transfers between devices  323 us (59%)
  matrix products  136 us (25%)
  other arithmetic  25.9 us (5%)
  local copies, waits for them, and re-layouts  19.8 us (4%)
  starting transfers between devices  19.1 us (4%)
  between operations  14.6 us (3%)
    reduce_scatter x1, waiting for transfers between devices, per_device(): lax.psum_scatter(contract_first(gathered, proj_grads).astype(jnp.bfloat16...  111 us
    ppermute x3, waiting for transfers between devices, per_device(): lax.ppermute(ring[-1], 'head', [(dev, (dev + 1) % 4) for dev in range(4)])  98.2 us
    reduce_scatter x1, waiting for transfers between devices, per_device(): lax.psum_scatter(partial_term.astype(jnp.bfloat16), 'head', scatter_dimen...  96.1 us
    dot_general x3, matrix products, contract_last(): lax.dot_general(left, right, (((1,), (1,)), ((), ())), preferred_element_...  41.6 us
    dot_general x1, matrix products, contract_first(): lax.dot_general(left, right, (((0,), (0,)), ((), ())), preferred_element_...  20.3 us
    sub x1, matrix products, attend(): expo = jnp.where(allowed, jnp.exp(masked - row_max), 0.0)  17.5 us
    ppermute x4, waiting for transfers between devices, passed_along(): return lax.ppermute(x, axis, pairs)  17.3 us
    convert_element_type x1, other arithmetic, attend(): dscores = (probs * (dprobs - center)).astype(jnp.bfloat16)  16.8 us
  transfers between devices with their start and end apart: 9, of which 7 were waited for; matrix products, arithmetic and copies ran while one was open for 12% of the time, Pallas kernels for 0%

profile of v1, /device:TPU:0, one launch (start us, length us, event | category | flops | bytes accessed | tf_op | source)
XLA Modules:
  0.0 537.4 jit_solution(17517577569129410471)
XLA Ops:
  7.2 3.1 collective-permute-start
  10.3 32.4 %collective-permute-done = bf16[512,1344]{0,1:T(8,128)(2,1)S(1)} collective-permute-done((bf16[512,1344]{0,1:T(8,128)(2,1)}, bf16[512,1344]{0,1:T(8,128)(2,1)S(1)}, u32[]{:S(2)}, u32[]{:S(2)}) %collective-permute-start) | collective-permute-done | bytes 1376288 | tf_op jit(solution)/shard_map/ppermute | solution.py:90
  42.7 33.3 %collective-permute-done.1 = bf16[512,1344]{0,1:T(8,128)(2,1)} collective-permute-done((bf16[512,1344]{0,1:T(8,128)(2,1)S(1)}, bf16[512,1344]{0,1:T(8,128)(2,1)}, u32[]{:S(2)}, u32[]{:S(2)}) %collective-permute-start.1) | collective-permute-done | bytes 1376288 | tf_op jit(solution)/shard_map/ppermute | solution.py:90
  76.0 32.6 %collective-permute-done.2 = bf16[512,1344]{0,1:T(8,128)(2,1)} collective-permute-done((bf16[512,1344]{0,1:T(8,128)(2,1)}, bf16[512,1344]{0,1:T(8,128)(2,1)}, u32[]{:S(2)}, u32[]{:S(2)}) %collective-permute-start.2) | collective-permute-done | bytes 1376288 | tf_op jit(solution)/shard_map/ppermute | solution.py:90
  108.5 1.4 constant_dynamic-update-slice_fusion.7
  110.0 1.4 constant_dynamic-update-slice_fusion.6
  111.5 0.1 constant_dynamic-update-slice_fusion.4
  111.6 1.6 constant_dynamic-update-slice_fusion.3
  113.2 1.5 constant_dynamic-update-slice_fusion.2
  115.0 0.2 slice-done.1
  115.2 3.0 fusion.46
  118.2 2.2 copy-done.8
  120.4 0.3 slice-done.3
  120.7 3.0 fusion.49
  123.7 0.1 pad_maximum_fusion.1
  123.8 2.3 collective-permute-start.3
  126.1 1.3 copy.35
  127.6 2.6 fusion.22
  130.2 10.8 %collective-permute-start.4 = (bf16[2,512,512]{2,1,0:T(8,128)(2,1)}, bf16[2,512,512]{2,1,0:T(8,128)(2,1)S(1)}, u32[]{:S(2)}, u32[]{:S(2)}) collective-permute-start(bf16[2,512,512]{2,1,0:T(8,128)(2,1)} %collective-permute-done.3), channel_id=1, source_target_pairs={{0,4},{4,8},{8,12},{12,16},{16,20},{20,24},{24,28},{1,5},{5,9},{9,... | collective-permute-start | bytes 3145736 | tf_op jit(solution)/shard_map/ppermute | solution.py:18
  141.0 11.1 %fusion.37 = bf16[512,1024]{1,0:T(8,128)(2,1)S(1)} fusion(bf16[5376,1024]{1,0:T(8,128)(2,1)} %param.7, bf16[512,10752]{0,1:T(8,128)(2,1)} %copy-done.8, s32[]{:T(128)S(6)} %select_n.27), kind=kOutput, calls=%fused_computation.54 | convolution fusion | flops 5637668864 | bytes 17563652 | tf_op jit(solution)/shard_map/dot_general | solution.py:94
  152.1 1.3 copy.34
  153.4 1.4 maximum_maximum_fusion
  154.8 1.4 fusion.60
  156.2 0.4 reshape_squeeze.6
  156.6 1.0 copy.22
  157.6 2.8 reshape_squeeze.7
  160.4 17.5 %fusion.62 = (f32[4,2,512]{2,1,0:T(2,128)S(1)}, f32[4,2,512,1536]{2,3,1,0:T(8,128)}) fusion(pred[512,1536]{0,1:T(8,128)(4,1)} %fusion.22, bf16[1536,4,128,1]{0,2,3,1:T(8,128)(2,1)S(1)} %copy.22, bf16[512,4,2,128]{0,3,2,1:T(8,128)(2,1)} %bitcast.74), kind=kOutput, calls=%fused_computation.84 | convolution fusion | flops 1642071552 | bytes 28590080 | tf_op jit(solution)/shard_map/sub | solution.py:58
  177.9 12.6 %fusion.5 = f32[4,1536,128,1]{1,2,3,0:T(8,128)} fusion(bf16[512,4,2,128]{0,3,2,1:T(8,128)(2,1)} %bitcast.77, f32[4,2,512,1536]{2,3,1,0:T(8,128)} %get-tuple-element.11, f32[4,2,512]{2,1,0:T(2,128)S(1)} %get-tuple-element.10), kind=kOutput, calls=%fused_computation.10 | convolution fusion | flops 1623195648 | bytes 29376512 | tf_op jit(solution)/shard_map/kgac,akgd->ckd/dot_general | solution.py:78
  190.5 16.6 %fusion.1 = (f32[4,2,512]{2,1,0:T(2,128)S(1)}, f32[4,1536,512,2]{2,1,3,0:T(8,128)}) fusion(f32[4,2,512,1536]{2,3,1,0:T(8,128)} %get-tuple-element.11, f32[4,2,512]{2,1,0:T(2,128)S(1)} %get-tuple-element.10, bf16[512,4,2,128]{0,3,2,1:T(8,128)(2,1)S(1)} %bitcast.78, bf16[1536,4,128,1]{2,1,0,3:T(4,128)(2,1)S(1)} %bitcast.76), kind=kOutput, calls=%fused_computation.3 | convolution fusion | flops 1629483008 | bytes 52985856 | tf_op jit(solution)/shard_map/akgd,ckd->kgac/dot_general | solution.py:60
  207.1 16.8 %fusion.3 = bf16[4,2,512,1536]{2,3,1,0:T(8,128)(2,1)S(1)} fusion(f32[4,1536,512,2]{2,1,3,0:T(8,128)} %get-tuple-element.13, f32[4,2,512]{2,1,0:T(2,128)S(1)} %get-tuple-element.12, f32[4,2,512,1536]{2,3,1,0:T(8,128)} %get-tuple-element.11, f32[4,2,512]{2,1,0:T(2,128)S(1)} %get-tuple-element.10), kind=kLoop, calls=%fused_computation.5 | loop fusion | flops 25165824 | bytes 62947328 | tf_op jit(solution)/shard_map/convert_element_type | solution.py:64
  223.9 7.0 %fusion.19 = f32[4,128,1536]{2,1,0:T(8,128)} fusion(bf16[512,4,2,128]{0,3,2,1:T(8,128)(2,1)} %bitcast.75, bf16[4,2,512,1536]{2,3,1,0:T(8,128)(2,1)S(1)} %fusion.3), kind=kOutput, calls=%fused_computation.33 | convolution fusion | flops 1611399168 | bytes 16777216 | tf_op jit(solution)/shard_map/kgac,akgd->ckd/dot_general | solution.py:75
  231.0 1.8 fusion.29
  232.8 1.6 collective-permute-start.5
  234.4 5.3 collective-permute-done.5
  239.7 0.4 fusion.25
  240.0 1.3 collective-permute-start.6
  241.3 2.8 multiply_convert_fusion.1
  244.1 12.0 %collective-permute-done.6 = bf16[2,512,512]{1,2,0:T(8,128)(2,1)S(1)} collective-permute-done((bf16[2,512,512]{1,2,0:T(8,128)(2,1)S(1)}, bf16[2,512,512]{1,2,0:T(8,128)(2,1)S(1)}, u32[]{:S(2)}, u32[]{:S(2)}) %collective-permute-start.6) | collective-permute-done | bytes 1048608 | tf_op jit(solution)/shard_map/ppermute | solution.py:18
  256.1 0.4 fusion.28
  256.6 20.3 %convolution_convert_fusion = bf16[5376,2048]{1,0:T(8,128)(2,1)} fusion(bf16[512,10752]{0,1:T(8,128)(2,1)} %copy-done.8, s32[]{:T(128)S(6)} %select_n.27, bf16[512,512]{0,1:T(8,128)(2,1)S(1)} %get-tuple-element.9, bf16[512,512]{0,1:T(8,128)(2,1)S(1)} %get-tuple-element.8, bf16[512,1024]{0,1:T(8,128)(2,1)S(1)} %bitcast.79), kind=kOutput, calls=%fused_computation.8 | convolution fusion | flops 11291590656 | bytes 29622276 | tf_op jit(solution)/shard_map/dot_general | solution.py:28
  277.0 12.9 %fusion.63 = f32[512,5376]{0,1:T(8,128)} fusion(bf16[5376,1024]{1,0:T(8,128)(2,1)} %param.7, bf16[512,1024]{0,1:T(8,128)(2,1)S(1)} %bitcast.80), kind=kOutput, calls=%fused_computation.85 | convolution fusion | flops 5637144576 | bytes 23068672 | tf_op jit(solution)/shard_map/dot_general | solution.py:22
  289.9 9.4 %fusion.59 = f32[512,5376]{0,1:T(8,128)} fusion(bf16[5376,512]{1,0:T(8,128)(2,1)} %param.8, bf16[2,512,512]{1,2,0:T(8,128)(2,1)S(1)} %fusion.28), kind=kOutput, calls=%fused_computation.81 | convolution fusion | flops 2818572288 | bytes 17039360 | tf_op jit(solution)/shard_map/dot_general | solution.py:22
  299.3 19.3 %add_convert_fusion = bf16[512,5376]{0,1:T(8,128)(2,1)} fusion(f32[512,5376]{0,1:T(8,128)} %fusion.63, f32[512,5376]{0,1:T(8,128)} %fusion.59, bf16[5376,512]{1,0:T(8,128)(2,1)} %param.9, bf16[2,512,512]{1,2,0:T(8,128)(2,1)S(1)} %fusion.28), kind=kOutput, calls=%fused_computation.16 | convolution fusion | flops 2826829824 | bytes 33554432 | tf_op jit(solution)/shard_map/dot_general | solution.py:22
  318.6 110.9 %reduce-scatter.5.cloned.1.call-done = bf16[672,2048]{1,0:T(8,128)(2,1)} async-done(((bf16[5376,2048]{1,0:T(8,128)(2,1)}), bf16[672,2048]{1,0:T(8,128)(2,1)}) %reduce-scatter.5.cloned.1.call-update) | async-done | bytes 2752528 | tf_op jit(solution)/shard_map/reduce_scatter | solution.py:137
  429.5 2.4 multiply_convert_fusion
  431.9 1.2 slice.54
  433.1 1.2 fusion.61
  434.3 96.1 %reduce-scatter.3.cloned.1.call-done = bf16[512,1344]{0,1:T(8,128)(2,1)} async-done(((bf16[512,5376]{0,1:T(8,128)(2,1)}), bf16[512,1344]{0,1:T(8,128)(2,1)}) %reduce-scatter.3.cloned.1.call-update) | async-done | bytes 1376272 | tf_op jit(solution)/shard_map/reduce_scatter | solution.py:133
  (43 shorter events, 0.7 us)
Async XLA Ops:
  7.2 104.3 %copy-start.4 = (bf16[512,1344]{0,1:T(8,128)(2,1)S(1)}, bf16[512,1344]{0,1:T(8,128)(2,1)}, u32[]{:S(2)}) copy-start(bf16[512,1344]{0,1:T(8,128)(2,1)} %param.6) | copy-start | bytes 4128772
  7.2 422.3 %reduce-scatter.5.cloned.1.call-start = ((), (), s32[]{:S(2)}) async-start(), calls=%async_computation.3 | async-start | bytes 24772608 | tf_op jit(solution)/shard_map/reduce_scatter | solution.py:137
  7.2 35.5 %collective-permute-start = (bf16[512,1344]{0,1:T(8,128)(2,1)}, bf16[512,1344]{0,1:T(8,128)(2,1)S(1)}, u32[]{:S(2)}, u32[]{:S(2)}) collective-permute-start(bf16[512,1344]{0,1:T(8,128)(2,1)} %param.6), channel_id=1, source_target_pairs={{0,1},{1,2},{2,3},{3,0},{4,5},{5,6},{6,7},{7,4},{8,9},{9,10},{10,1... | collective-permute-start | bytes 4128776 | tf_op jit(solution)/shard_map/ppermute | solution.py:90
  42.7 33.3 %collective-permute-start.1 = (bf16[512,1344]{0,1:T(8,128)(2,1)S(1)}, bf16[512,1344]{0,1:T(8,128)(2,1)}, u32[]{:S(2)}, u32[]{:S(2)}) collective-permute-start(bf16[512,1344]{0,1:T(8,128)(2,1)S(1)} %collective-permute-done), channel_id=1, source_target_pairs={{0,1},{1,2},{2,3},{3,0},{4,5},{5,6},{6,7},{7,4},{8,9},{9,10},{10,1... | collective-permute-start | bytes 4128776 | tf_op jit(solution)/shard_map/ppermute | solution.py:90
  76.0 32.6 %collective-permute-start.2 = (bf16[512,1344]{0,1:T(8,128)(2,1)}, bf16[512,1344]{0,1:T(8,128)(2,1)}, u32[]{:S(2)}, u32[]{:S(2)}) collective-permute-start(bf16[512,1344]{0,1:T(8,128)(2,1)} %collective-permute-done.1), channel_id=1, source_target_pairs={{0,1},{1,2},{2,3},{3,0},{4,5},{5,6},{6,7},{7,4},{8,9},{9,10},{10,1... | collective-permute-start | bytes 4128776 | tf_op jit(solution)/shard_map/ppermute | solution.py:90
  111.5 3.5 slice-start
  113.2 2.0 slice-start.1
  114.9 5.5 %slice-start.2 = ((s8[5505024]{0:T(1024)(128)(4,1)}), s8[4194304]{0:T(1024)(128)(4,1)S(1)}, s32[]{:S(2)}) async-start(s8[5505024]{0:T(1024)(128)(4,1)} %bitcast.71), calls=%async_computation.6 | async-start | bytes 8388608
  115.2 5.2 copy-start.8
  115.2 5.5 %slice-start.3 = ((s8[5505024]{0:T(1024)(128)(4,1)}), s8[1310720]{0:T(1024)(128)(4,1)S(1)}, s32[]{:S(2)}) async-start(s8[5505024]{0:T(1024)(128)(4,1)} %bitcast.71), calls=%async_computation.7 | async-start | bytes 2621440
  120.7 5.5 %copy-start.5 = (bf16[512,1024]{1,0:T(8,128)(2,1)S(1)}, bf16[512,1024]{1,0:T(8,128)(2,1)}, u32[]{:S(2)}) copy-start(bf16[512,1024]{1,0:T(8,128)(2,1)} %param.10) | copy-start | bytes 3145732
  120.7 6.8 %copy-start.9 = (s32[4096]{0:T(1024)S(1)}, s32[4096]{0:T(1024)}, u32[]{:S(2)}) copy-start(s32[4096]{0:T(1024)} %param.11) | copy-start | bytes 49156
  123.8 6.4 %collective-permute-start.3 = (bf16[2,512,512]{2,1,0:T(8,128)(2,1)S(1)}, bf16[2,512,512]{2,1,0:T(8,128)(2,1)}, u32[]{:S(2)}, u32[]{:S(2)}) collective-permute-start(bf16[2,512,512]{2,1,0:T(8,128)(2,1)S(1)} %pad_maximum_fusion.1), channel_id=1, source_target_pairs={{0,4},{4,8},{8,12},{12,16},{16,20},{20,24},{24,28},{1,5},{5,9},{9,... | collective-permute-start | bytes 3145736 | tf_op jit(solution)/shard_map/ppermute | solution.py:18
  130.2 23.2 %collective-permute-start.4 = (bf16[2,512,512]{2,1,0:T(8,128)(2,1)}, bf16[2,512,512]{2,1,0:T(8,128)(2,1)S(1)}, u32[]{:S(2)}, u32[]{:S(2)}) collective-permute-start(bf16[2,512,512]{2,1,0:T(8,128)(2,1)} %collective-permute-done.3), channel_id=1, source_target_pairs={{0,4},{4,8},{8,12},{12,16},{16,20},{20,24},{24,28},{1,5},{5,9},{9,... | collective-permute-start | bytes 3145736 | tf_op jit(solution)/shard_map/ppermute | solution.py:18
  157.6 20.3 %copy-start.2 = (bf16[1536,4,128,1]{0,2,3,1:T(8,128)(2,1)}, bf16[1536,4,128,1]{0,2,3,1:T(8,128)(2,1)S(1)}, u32[]{:S(2)}) copy-start(bf16[1536,4,128,1]{0,2,3,1:T(8,128)(2,1)S(1)} %copy.22) | copy-start | bytes 4718596
  177.9 12.6 %copy-start.6 = (bf16[512,1024]{0,1:T(8,128)(2,1)S(1)}, bf16[512,1024]{0,1:T(8,128)(2,1)}, u32[]{:S(2)}) copy-start(bf16[512,1024]{0,1:T(8,128)(2,1)} %copy.35) | copy-start | bytes 3145732
  231.0 8.7 %copy-start = (f32[4,128,1536]{2,1,0:T(8,128)S(1)}, f32[4,128,1536]{2,1,0:T(8,128)}, u32[]{:S(2)}) copy-start(f32[4,128,1536]{2,1,0:T(8,128)} %fusion.19) | copy-start | bytes 9437188
  231.0 8.7 %copy-start.1 = (f32[4,1536,128,1]{1,2,3,0:T(8,128)S(1)}, f32[4,1536,128,1]{1,2,3,0:T(8,128)}, u32[]{:S(2)}) copy-start(f32[4,1536,128,1]{1,2,3,0:T(8,128)} %fusion.5) | copy-start | bytes 9437188
  232.8 8.5 %copy-start.3 = (bf16[1536,4,128,1]{0,2,3,1:T(8,128)(2,1)S(1)}, bf16[1536,4,128,1]{0,2,3,1:T(8,128)(2,1)}, u32[]{:S(2)}) copy-start(bf16[1536,4,128,1]{0,2,3,1:T(8,128)(2,1)} %copy-done.2) | copy-start | bytes 4718596
  232.8 6.8 %collective-permute-start.5 = (bf16[2,512,512]{1,2,0:T(8,128)(2,1)S(1)}, bf16[2,512,512]{1,2,0:T(8,128)(2,1)S(1)}, u32[]{:S(2)}, u32[]{:S(2)}) collective-permute-start(bf16[2,512,512]{1,2,0:T(8,128)(2,1)S(1)} %fusion.29), channel_id=1, source_target_pairs={{4,0},{8,4},{12,8},{16,12},{20,16},{24,20},{28,24},{5,1},{9,5},{13... | collective-permute-start | bytes 3145736 | tf_op jit(solution)/shard_map/ppermute | solution.py:18
  240.0 16.1 %collective-permute-start.6 = (bf16[2,512,512]{1,2,0:T(8,128)(2,1)S(1)}, bf16[2,512,512]{1,2,0:T(8,128)(2,1)S(1)}, u32[]{:S(2)}, u32[]{:S(2)}) collective-permute-start(bf16[2,512,512]{1,2,0:T(8,128)(2,1)S(1)} %fusion.25), channel_id=1, source_target_pairs={{4,0},{8,4},{12,8},{16,12},{20,16},{24,20},{28,24},{5,1},{9,5},{13... | collective-permute-start | bytes 3145736 | tf_op jit(solution)/shard_map/ppermute | solution.py:18
  244.1 12.5 %copy-start.7 = (bf16[4,128,2,512]{3,1,2,0:T(8,128)(2,1)S(1)}, bf16[4,128,2,512]{3,1,2,0:T(8,128)(2,1)}, u32[]{:S(2)}) copy-start(bf16[4,128,2,512]{3,1,2,0:T(8,128)(2,1)} %multiply_convert_fusion.1) | copy-start | bytes 3145732
  276.9 253.4 %reduce-scatter.3.cloned.1.call-start = ((), (), s32[]{:S(2)}) async-start(), calls=%async_computation.2 | async-start | bytes 6881280 | tf_op jit(solution)/shard_map/reduce_scatter | solution.py:133
Sparse Core Ops, SparseCore 0:
  277.1 152.3 reduce-scatter.4
  432.3 97.9 reduce-scatter.2
